TPU v7x, 32 devices: a whole 2x2x4 slice. The times are simulated.
32 devices in a mesh: ctx: 8 (over y, x, core), tp: 4 (over z).
Axes of the slice: x: 2, y: 2, z: 4, core: 2. Of those that a mesh axis runs over, the one named last changes fastest.
Arguments:
- tokens: bfloat16 [4096, 4096], P(('ctx', 'tp')), may hold values from -6 to 6
- spike_query: int32 [4096, 32], P('ctx', 'tp'), may hold values 0 or 1
- spike_key: int32 [4096, 32], P('ctx', 'tp'), may hold values 0 or 1
- qkv_weight: bfloat16 [4096, 3, 4096], P(None, None, 'tp'), may hold values from -0.09375 to 0.09375
- qkv_blocks: int32 [3, 32, 32], P(None, None, 'tp'), may hold values 0 or 1
- out_weight: bfloat16 [4096, 4096], P('tp'), may hold values from -0.09375 to 0.09375
- out_blocks: int32 [32, 32], P('tp'), may hold values 0 or 1
- cotangent: bfloat16 [4096, 4096], P(('ctx', 'tp')), may hold values from -6 to 6
Outputs:
- layer_out: bfloat16 [4096, 4096], P(('ctx', 'tp'))
- token_grad: bfloat16 [4096, 4096], P(('ctx', 'tp'))
- qkv_grad: float32 [4096, 3, 4096], P('ctx', None, 'tp')
- out_grad: float32 [4096, 4096], P('tp', 'ctx')
All inputs are finite; a program needn't handle non-finite values. No bound on the sum of `spike_query` or of `spike_key` or of `qkv_blocks` or of `out_blocks` on one device may be relied on, other than what follows from the above.
Results may differ from a plain program's by a relative error of at most 0.014.
Values may be sent and summed in bfloat16 or wider, within the bound.
No kernel may reach another device: no remote copies, remote signals or barrier semaphores. Data moves between devices by JAX's collectives and lax.ppermute only.
A program may use at most 320 MiB of HBM per device.

v0:
```python
import math
import jax
import jax.numpy as jnp
from jax import lax
from jax.sharding import PartitionSpec as P

BLOCK = 128
EPSILON = 1e-05


def carried_in(value, axis, join, neutral):
    place = lax.axis_index(axis)
    gathered = lax.all_gather(value.astype(jnp.bfloat16), axis)
    state = jnp.zeros_like(value) + jnp.asarray(neutral, value.dtype)

    def carried_one(lap, state):
        return join(state, lax.dynamic_index_in_dim(gathered, lap, 0, False).astype(value.dtype))

    return lax.fori_loop(0, place, carried_one, state)


def entering(value, axis, join, neutral):
    count = lax.axis_size(axis)
    place = lax.axis_index(axis)
    ahead = count - 1 - place
    gathered = lax.all_gather(
        value.astype(jnp.bfloat16 if value.dtype == jnp.float32 else value.dtype), axis
    )
    state = jnp.zeros_like(value) + jnp.asarray(neutral, value.dtype)

    def entering_one(lap, state):
        source = count - 1 - lap
        return join(state, lax.dynamic_index_in_dim(gathered, source, 0, False).astype(value.dtype))

    return lax.fori_loop(0, ahead, entering_one, state)


def expand_blocks(blocks):
    row_blocks, col_blocks = blocks.shape
    spread = jnp.broadcast_to(
        blocks.astype(jnp.bfloat16)[:, None, :, None], (row_blocks, BLOCK, col_blocks, BLOCK)
    )
    return spread.reshape(row_blocks * BLOCK, col_blocks * BLOCK)


def qkv_keep_table(qkv_blocks):
    tables = [expand_blocks(qkv_blocks[projection]) for projection in range(3)]
    return jnp.stack(tables, axis=1)


def add_states(earlier, following):
    return earlier + following


def on_device(
    tokens, spike_query, spike_key, qkv_weight, qkv_blocks, out_weight, out_blocks, cotangent
):
    model_width = tokens.shape[1]
    block_rows = spike_query.shape[0]
    local_heads = spike_query.shape[1]
    features = qkv_weight.shape[2]
    head_width = features // local_heads
    row_blocks = model_width // BLOCK
    col_blocks = features // BLOCK
    highest = lax.Precision.HIGHEST
    qkv_mask = jnp.transpose(qkv_blocks, (1, 0, 2)).astype(jnp.bfloat16)
    qkv_used = (
        qkv_weight.reshape(row_blocks, BLOCK, 3, col_blocks, BLOCK) * qkv_mask[:, None, :, :, None]
    ).reshape(model_width, 3 * features)
    out_used = (
        out_weight.reshape(col_blocks, BLOCK, row_blocks, BLOCK)
        * out_blocks.astype(jnp.bfloat16)[:, None, :, None]
    ).reshape(features, model_width)
    gathered = lax.all_gather(tokens, "tp", axis=0, tiled=True)
    projected = jnp.dot(gathered, qkv_used, preferred_element_type=jnp.float32).astype(jnp.bfloat16)
    projected = projected.reshape(block_rows, 3, local_heads, head_width)
    query_spikes = spike_query.astype(jnp.bfloat16)[:, :, None]
    key_spikes = spike_key.astype(jnp.bfloat16)[:, :, None]
    query_spiked = projected[:, 0] * query_spikes
    key_spiked = projected[:, 1] * key_spikes
    values = projected[:, 2]
    query_wide = query_spiked.astype(jnp.float32)
    key_wide = key_spiked.astype(jnp.float32)
    local_state = jnp.einsum("shd,she->hde", key_spiked, values, preferred_element_type=jnp.float32)
    zeros_state = jnp.zeros_like(local_state)
    prior_state = carried_in(local_state, "ctx", add_states, zeros_state)
    positions = lax.iota(jnp.int32, block_rows)
    causal_keep = positions[:, None] >= positions[None, :]
    scores = jnp.einsum(
        "thd,shd->hts", query_spiked, key_spiked, preferred_element_type=jnp.float32
    )
    scores = jnp.where(causal_keep, scores, 0.0).astype(jnp.bfloat16)
    mixed_rows = jnp.einsum("hts,she->the", scores, values, preferred_element_type=jnp.float32)
    mixed_rows = mixed_rows + jnp.einsum("thd,hde->the", query_wide, prior_state, precision=highest)
    inv_rms = lax.rsqrt(jnp.mean(mixed_rows * mixed_rows, axis=-1, keepdims=True) + EPSILON)
    normed = mixed_rows * inv_rms
    attended = normed.astype(jnp.bfloat16).reshape(block_rows, features)
    head_sum = lax.psum_scatter(
        jnp.dot(attended, out_used, preferred_element_type=jnp.float32).astype(jnp.bfloat16),
        "tp",
        scatter_dimension=0,
        tiled=True,
    ).astype(jnp.float32)
    layer_out = (tokens.astype(jnp.float32) + head_sum).astype(jnp.bfloat16)
    grad_rows = lax.all_gather(cotangent, "tp", axis=0, tiled=True)
    ctx_count = lax.axis_size("ctx")
    ctx_place = lax.axis_index("ctx")
    slice_rows = model_width // ctx_count
    slice_blocks = slice_rows // BLOCK
    norm_factor = 1.0 / math.sqrt(block_rows * ctx_count)
    out_part = jnp.einsum("tm,tf->mf", grad_rows, attended, preferred_element_type=jnp.float32)
    out_sum = lax.psum_scatter(
        out_part.astype(jnp.bfloat16), "ctx", scatter_dimension=0, tiled=True
    ).astype(jnp.float32)
    out_keep = lax.dynamic_slice_in_dim(out_blocks, ctx_place * slice_blocks, slice_blocks, 1)
    out_keep = jnp.broadcast_to(
        jnp.transpose(out_keep).astype(jnp.float32)[:, None, :, None],
        (slice_blocks, BLOCK, col_blocks, BLOCK),
    ).reshape(slice_rows, features)
    out_grad = jnp.transpose(out_sum * out_keep * norm_factor)
    grad_attended = jnp.einsum("tm,fm->tf", grad_rows, out_used, preferred_element_type=jnp.float32)
    grad_attended = grad_attended.reshape(block_rows, local_heads, head_width)
    inner_mean = jnp.mean(grad_attended * normed, axis=-1, keepdims=True)
    grad_mixed = inv_rms * (grad_attended - normed * inner_mean)
    grad_low = grad_mixed.astype(jnp.bfloat16)
    local_adjoint = jnp.einsum("thd,the->hde", query_wide, grad_mixed, precision=highest)
    after_state = entering(local_adjoint, "ctx", add_states, zeros_state)
    adjoint_scores = jnp.einsum(
        "the,she->hts", grad_low, values, preferred_element_type=jnp.float32
    )
    adjoint_scores = jnp.where(causal_keep, adjoint_scores, 0.0).astype(jnp.bfloat16)
    grad_query = jnp.einsum(
        "hts,shd->thd", adjoint_scores, key_spiked, preferred_element_type=jnp.float32
    )
    grad_query = grad_query + jnp.einsum("the,hde->thd", grad_mixed, prior_state, precision=highest)
    grad_key = jnp.einsum(
        "hts,thd->shd", adjoint_scores, query_spiked, preferred_element_type=jnp.float32
    )
    grad_key = grad_key + jnp.einsum(
        "she,hde->shd", values.astype(jnp.float32), after_state, precision=highest
    )
    grad_value = jnp.einsum("hts,the->she", scores, grad_low, preferred_element_type=jnp.float32)
    grad_value = grad_value + jnp.einsum("shd,hde->she", key_wide, after_state, precision=highest)
    grad_proj = jnp.stack(
        [
            (grad_query * query_spikes.astype(jnp.float32)).astype(jnp.bfloat16),
            (grad_key * key_spikes.astype(jnp.float32)).astype(jnp.bfloat16),
            grad_value.astype(jnp.bfloat16),
        ],
        axis=1,
    ).reshape(block_rows, 3 * features)
    qkv_part = jnp.einsum("tm,tc->mc", gathered, grad_proj, preferred_element_type=jnp.float32)
    qkv_sum = lax.psum_scatter(
        qkv_part.astype(jnp.bfloat16), "ctx", scatter_dimension=0, tiled=True
    ).astype(jnp.float32)
    qkv_keep = lax.dynamic_slice_in_dim(qkv_mask, ctx_place * slice_blocks, slice_blocks, 0)
    qkv_keep = jnp.broadcast_to(
        qkv_keep.astype(jnp.float32)[:, None, :, :, None],
        (slice_blocks, BLOCK, 3, col_blocks, BLOCK),
    ).reshape(slice_rows, 3, features)
    qkv_grad = qkv_sum.reshape(slice_rows, 3, features) * qkv_keep * norm_factor
    token_sum = lax.psum_scatter(
        jnp.einsum("tc,mc->tm", grad_proj, qkv_used, preferred_element_type=jnp.float32).astype(
            jnp.bfloat16
        ),
        "tp",
        scatter_dimension=0,
        tiled=True,
    ).astype(jnp.float32)
    token_grad = (cotangent.astype(jnp.float32) + token_sum).astype(jnp.bfloat16)
    return (layer_out, token_grad, qkv_grad, out_grad)


def solution(mesh):
    placed = (
        P(("ctx", "tp"), None),
        P("ctx", "tp"),
        P("ctx", "tp"),
        P(None, None, "tp"),
        P(None, None, "tp"),
        P("tp", None),
        P("tp", None),
        P(("ctx", "tp"), None),
    )
    return jax.shard_map(
        on_device,
        mesh=mesh,
        in_specs=placed,
        out_specs=(
            P(("ctx", "tp"), None),
            P(("ctx", "tp"), None),
            P("ctx", None, "tp"),
            P("tp", "ctx"),
        ),
        check_vma=False,
    )
```

profile of v0, /device:TPU:0, one launch (start us, length us, event | category | flops | bytes accessed | tf_op | source)
XLA Modules:
  0.0 764.5 jit_solution(3684629579513583311)
XLA Ops:
  8.8 8.7 %mul.111 = bf16[32,128,3,8,128]{4,3,2,1,0:T(8,128)(2,1)} broadcast(bf16[32,3,8]{2,1,0:T(4,128)(2,1)S(1)} %copy.47), dimensions={0,2,3} | broadcast | bytes 25167360 | tf_op jit(solution)/shard_map/mul | solution.py:68
  17.5 37.4 %mul.112 = bf16[4096,3072]{1,0:T(8,128)(2,1)} reshape(bf16[32,128,3,8,128]{4,3,2,1,0:T(8,128)(2,1)} %mul.111) | data formatting | bytes 50331648 | tf_op jit(solution)/shard_map/mul | solution.py:68
  54.9 31.5 %copy.48 = bf16[4096,3072]{0,1:T(8,128)(2,1)} copy(bf16[4096,3072]{1,0:T(8,128)(2,1)} %mul.112) | data formatting | bytes 50331648 | tf_op jit(solution)/shard_map/mul | solution.py:68
  86.4 33.6 %copy.46 = bf16[4096,3,1024]{0,2,1:T(8,128)(2,1)} copy(bf16[4096,3,1024]{2,0,1:T(8,128)(2,1)} %param.15) | data formatting | bytes 50331648 | tf_op args[3]
  120.0 25.4 %bitcast_multiply_fusion = bf16[4096,3072]{0,1:T(8,128)(2,1)} fusion(bf16[4096,3072]{0,1:T(8,128)(2,1)} %copy.48, bf16[4096,3,1024]{0,2,1:T(8,128)(2,1)} %copy.46), kind=kLoop, calls=%fused_computation.2 | loop fusion | flops 12582912 | bytes 75497472 | tf_op jit(solution)/shard_map/mul | solution.py:68
  145.4 18.2 %convolution_convert_fusion.2 = bf16[3072,512]{1,0:T(8,128)(2,1)S(1)} fusion(bf16[4096,3072]{0,1:T(8,128)(2,1)} %bitcast_multiply_fusion, bf16[512,4096]{1,0:T(8,128)(2,1)} %all-gather.7.cloned.1.call-done), kind=kOutput, calls=%fused_computation.11 | convolution fusion | flops 12886474752 | bytes 32505856 | tf_op jit(solution)/shard_map/dot_general | solution.py:75
  163.6 1.5 convolution_convert_fusion.3
  166.1 1.4 select_convert_fusion.1
  167.5 2.0 copy-done.4
  169.5 2.8 fusion.12
  172.3 23.8 %all-gather.11.cloned.1.call-done = bf16[64,128,128]{2,1,0:T(8,128)(2,1)} async-done(((bf16[8,128,128]{2,1,0:T(8,128)(2,1)}), bf16[64,128,128]{2,1,0:T(8,128)(2,1)}) %all-gather.11.cloned.1.call-update) | async-done | bytes 2097168 | tf_op jit(solution)/shard_map/all_gather | solution.py:13
  196.7 3.1 fusion.5
  199.8 78.7 %all-gather.9.cloned.1.call-done = bf16[512,4096]{1,0:T(8,128)(2,1)} async-done(((bf16[128,4096]{1,0:T(8,128)(2,1)}), bf16[512,4096]{1,0:T(8,128)(2,1)}) %all-gather.9.cloned.1.call-update) | async-done | bytes 4194320 | tf_op jit(solution)/shard_map/all_gather | solution.py:105
  278.4 1.1 mul.121
  279.6 12.4 %multiply_reduce_fusion = (f32[512,8]{0,1:T(8,128)S(1)}, f32[1024,512]{1,0:T(8,128)S(1)}) fusion(f32[8,128,512]{2,1,0:T(8,128)S(1)} %get-tuple-element.108, f32[512,8]{0,1:T(8,128)S(1)} %add_rsqrt_fusion, bf16[512,4096]{1,0:T(8,128)(2,1)} %all-gather.9.cloned.1.call-done, bf16[1024,4096]{1,0:T(8,128)(2,1)} %param.17, bf16[128,8,32,128]{3,2,1,0:T(8,128)(2,1)S(1)} %bitcast.142), kind=kOutput, calls=%fused_computation.27 | convolution fusion | flops 4300730368 | bytes 25198592 | tf_op jit(solution)/shard_map/tm,fm->tf/dot_general | solution.py:121
  292.1 3.2 subtract_multiply_fusion
  295.2 3.1 convolution_convert_fusion.4
  298.6 13.4 %convolution_convert_fusion.1 = bf16[512,4096]{1,0:T(8,128)(2,1)} fusion(bf16[512,1024]{0,1:T(8,128)(2,1)} %bitcast.159, bf16[1024,4096]{1,0:T(8,128)(2,1)} %param.17, bf16[128,8,32,128]{3,2,1,0:T(8,128)(2,1)} %bitcast.143), kind=kOutput, calls=%fused_computation.10 | convolution fusion | flops 4301258752 | bytes 22020096 | tf_op jit(solution)/shard_map/dot_general | solution.py:99
  312.1 8.8 %mul.111.clone = bf16[32,128,3,8,128]{1,0,4,3,2:T(8,128)(2,1)} broadcast(bf16[32,3,8]{0,2,1:T(8,128)(2,1)S(1)} %convert_bitcast_fusion.4), dimensions={0,2,3} | broadcast | bytes 25167360 | tf_op jit(solution)/shard_map/mul | solution.py:68
  320.9 37.5 %mul.132 = bf16[4096,3,1024]{0,2,1:T(8,128)(2,1)} reshape(bf16[32,128,3,8,128]{1,0,4,3,2:T(8,128)(2,1)} %mul.111.clone) | data formatting | bytes 50331648 | tf_op jit(solution)/shard_map/mul | solution.py:68
  358.4 28.7 %mul.133 = bf16[4096,3,1024]{0,2,1:T(8,128)(2,1)} multiply(bf16[4096,3,1024]{0,2,1:T(8,128)(2,1)} %copy.46, bf16[4096,3,1024]{0,2,1:T(8,128)(2,1)} %mul.132) | non-fusion elementwise | flops 12582912 | bytes 75497472 | tf_op jit(solution)/shard_map/mul | solution.py:68
  387.1 2.7 select_convert_fusion
  389.9 1.5 fusion.22
  391.4 2.9 fusion.8
  394.2 2.2 fusion.17
  397.2 2.0 fusion.13
  399.3 7.9 %while.23 = (s32[]{:T(128)}, f32[8,128,128]{2,1,0:T(8,128)S(1)}, s32[]{:T(128)}, bf16[8,8,128,128]{3,2,1,0:T(8,128)(2,1)}, s32[]{:T(128)}, /*index=5*/s32[]{:T(128)}, s32[]{:T(128)}, s32[]{:T(128)}) while((s32[]{:T(128)}, f32[8,128,128]{2,1,0:T(8,128)S(1)}, s32[]{:T(128)}, bf16[8,8,128,128]{3,2,1,0:T(8,128)(2,1)}, s32[]{:T(128)}, ...), condition=%wide.region_6.7_spmd, body=%wide.region_5.6_spmd.sunk | while | flops 262150 | bytes 1310863 | solution.py:35
  399.5 1.1 convert_add_fusion.5
  400.6 1.1 convert_add_fusion.5
  401.7 1.1 convert_add_fusion.5
  402.8 1.1 convert_add_fusion.5
  403.9 1.1 convert_add_fusion.5
  405.0 1.1 convert_add_fusion.5
  407.2 3.1 fusion.7
  410.3 2.4 fusion.9
  413.1 19.5 %convolution_convert_fusion = bf16[512,4096]{1,0:T(8,128)(2,1)} fusion(bf16[512,3072]{0,1:T(8,128)(2,1)S(1)} %bitcast.156, bf16[4096,3072]{0,1:T(8,128)(2,1)} %bitcast.144), kind=kOutput, calls=%fused_computation.9 | convolution fusion | flops 12886999040 | bytes 32505856 | tf_op jit(solution)/shard_map/tc,mc->tm/dot_general | solution.py:163
  432.9 10.5 %convert_bitcast_fusion.1 = bf16[4096,1024]{0,1:T(8,128)(2,1)} fusion(bf16[512,1024]{0,1:T(8,128)(2,1)} %bitcast.160, bf16[512,4096]{1,0:T(8,128)(2,1)} %all-gather.9.cloned.1.call-done), kind=kOutput, calls=%fused_computation.5 | convolution fusion | flops 4299161600 | bytes 13631488 | tf_op jit(solution)/shard_map/tm,tf->mf/dot_general | solution.py:111
  443.4 19.1 %convert_bitcast_fusion = bf16[4096,3072]{0,1:T(8,128)(2,1)} fusion(bf16[512,3072]{0,1:T(8,128)(2,1)S(1)} %bitcast.157, bf16[512,4096]{1,0:T(8,128)(2,1)} %all-gather.7.cloned.1.call-done), kind=kOutput, calls=%fused_computation.3 | convolution fusion | flops 12897484800 | bytes 32505856 | tf_op jit(solution)/shard_map/tm,tc->mc/dot_general | solution.py:152
  463.5 3.2 broadcast_in_dim.38
  466.7 7.2 reshape.76
  473.9 2.5 add_convert_fusion.2
  476.4 29.7 %reduce-scatter.7.cloned.1.call-done = bf16[128,4096]{1,0:T(8,128)(2,1)} async-done(((bf16[512,4096]{1,0:T(8,128)(2,1)}), bf16[128,4096]{1,0:T(8,128)(2,1)}) %reduce-scatter.7.cloned.1.call-update) | async-done | bytes 1048592 | tf_op jit(solution)/shard_map/reduce_scatter | solution.py:162
  506.1 2.4 add_convert_fusion
  508.5 72.8 %reduce-scatter.11.cloned.1.call-done = bf16[512,1024]{0,1:T(8,128)(2,1)} async-done(((bf16[4096,1024]{0,1:T(8,128)(2,1)}), bf16[512,1024]{0,1:T(8,128)(2,1)}) %reduce-scatter.11.cloned.1.call-update) | async-done | bytes 1048592 | tf_op jit(solution)/shard_map/reduce_scatter | solution.py:112
  581.7 2.9 fusion.2
  584.6 157.7 %reduce-scatter.9.cloned.1.call-done = bf16[512,3072]{0,1:T(8,128)(2,1)} async-done(((bf16[4096,3072]{0,1:T(8,128)(2,1)}), bf16[512,3072]{0,1:T(8,128)(2,1)}) %reduce-scatter.9.cloned.1.call-update) | async-done | bytes 3145744 | tf_op jit(solution)/shard_map/reduce_scatter | solution.py:153
  742.3 5.4 copy.64
  747.7 9.5 %multiply_multiply_fusion = f32[512,3,1024]{2,0,1:T(8,128)} fusion(f32[512,3,1024]{2,0,1:T(8,128)} %copy.64, f32[512,3,1024]{2,0,1:T(8,128)} %reshape.76), kind=kLoop, calls=%fused_computation.8 | loop fusion | flops 3145728 | bytes 18874368 | tf_op jit(solution)/shard_map/mul | solution.py:161
  (65 shorter events, 7.2 us)
Async XLA Ops:
  7.2 138.3 %all-gather.7.cloned.1.call-start = ((), (), s32[]{:S(2)}) async-start(), calls=%async_computation.4 | async-start | bytes 5242880 | tf_op jit(solution)/shard_map/all_gather | solution.py:74
  7.9 188.2 %all-gather.11.cloned.1.call-start = ((), (), s32[]{:S(2)}) async-start(), calls=%async_computation.10 | async-start | bytes 2359296 | tf_op jit(solution)/shard_map/all_gather | solution.py:13
  86.4 33.6 %copy-start.11 = (s32[512,8]{0,1:T(8,128)S(1)}, s32[512,8]{0,1:T(8,128)}, u32[]{:S(2)}) copy-start(s32[512,8]{0,1:T(8,128)} %param.13) | copy-start | bytes 49156
  86.4 33.6 %copy-start.12 = (s32[512,8]{0,1:T(8,128)S(1)}, s32[512,8]{0,1:T(8,128)}, u32[]{:S(2)}) copy-start(s32[512,8]{0,1:T(8,128)} %param.14) | copy-start | bytes 49156
  163.6 3.9 copy-start.1
  163.6 2.3 copy-start.13
  165.2 113.3 %all-gather.9.cloned.1.call-start = ((), (), s32[]{:S(2)}) async-start(), calls=%async_computation.6 | async-start | bytes 5242880 | tf_op jit(solution)/shard_map/all_gather | solution.py:105
  165.9 233.3 %all-gather.13.cloned.1.call-start = ((), (), s32[]{:S(2)}) async-start(), calls=%async_computation.11 | async-start | bytes 2359296 | tf_op jit(solution)/shard_map/all_gather | solution.py:26
  167.5 2.0 copy-start.4
  199.7 79.9 %copy-start.3 = (f32[8,128,512]{2,1,0:T(8,128)}, f32[8,128,512]{2,1,0:T(8,128)S(1)}, u32[]{:S(2)}) copy-start(f32[8,128,512]{2,1,0:T(8,128)S(1)} %get-tuple-element.108) | copy-start | bytes 6291460
  279.6 12.4 %copy-start = (bf16[8,128,32,128]{3,2,1,0:T(8,128)(2,1)}, bf16[8,128,32,128]{3,2,1,0:T(8,128)(2,1)S(1)}, u32[]{:S(2)}) copy-start(bf16[8,128,32,128]{3,2,1,0:T(8,128)(2,1)S(1)} %mul.121) | copy-start | bytes 25165828
  298.4 175.5 %reduce-scatter.5.cloned.1.call-start = ((), (), s32[]{:S(2)}) async-start(), calls=%async_computation.5 | async-start | bytes 5242880 | tf_op jit(solution)/shard_map/reduce_scatter | solution.py:98
  312.0 194.0 %reduce-scatter.7.cloned.1.call-start = ((), (), s32[]{:S(2)}) async-start(), calls=%async_computation.7 | async-start | bytes 5242880 | tf_op jit(solution)/shard_map/reduce_scatter | solution.py:162
  387.1 2.7 copy-start.2
  394.2 2.9 copy-start.5
  407.1 3.2 copy-start.6
  410.3 2.5 copy-start.9
  432.6 148.7 %reduce-scatter.11.cloned.1.call-start = ((), (), s32[]{:S(2)}) async-start(), calls=%async_computation.9 | async-start | bytes 9437184 | tf_op jit(solution)/shard_map/reduce_scatter | solution.py:112
  443.4 298.9 %reduce-scatter.9.cloned.1.call-start = ((), (), s32[]{:S(2)}) async-start(), calls=%async_computation.8 | async-start | bytes 28311552 | tf_op jit(solution)/shard_map/reduce_scatter | solution.py:153
  462.6 0.7 copy-start.10
  466.7 7.2 copy-start.14
  466.7 7.2 copy-start.7
  473.8 32.3 %copy-start.8 = (bf16[128,4096]{1,0:T(8,128)(2,1)S(1)}, bf16[128,4096]{1,0:T(8,128)(2,1)}, u32[]{:S(2)}) copy-start(bf16[128,4096]{1,0:T(8,128)(2,1)} %param.19) | copy-start | bytes 3145732
Sparse Core Ops, SparseCore 0:
  9.6 83.4 all-gather.6
  165.3 30.7 all-gather.10
  197.6 80.7 all-gather.8
  298.5 26.4 all-gather.12
  327.1 76.8 reduce-scatter.4
  432.7 73.3 reduce-scatter.6
  509.5 71.7 reduce-scatter.10
  585.4 156.8 reduce-scatter.8
where the time goes:
time: 775 us; the launch traced here: 765 us
  waiting for transfers between devices  364 us (47%)
  local copies, waits for them, and re-layouts  179 us (23%)
  matrix products  122 us (16%)
  other arithmetic  83.5 us (11%)
  between operations  14.9 us (2%)
    reduce_scatter x1, waiting for transfers between devices, on_device(): lax.psum_scatter(qkv_part.astype(jnp.bfloat16), 'ctx', scatter_dimension=...  158 us
    mul x5, local copies, waits for them, and re-layouts, on_device(): qkv_weight.reshape(row_blocks, BLOCK, 3, col_blocks, BLOCK)  124 us
    all_gather x1, waiting for transfers between devices, on_device(): grad_rows = lax.all_gather(cotangent, 'tp', axis=0, tiled=True)  78.7 us
    reduce_scatter x1, waiting for transfers between devices, on_device(): lax.psum_scatter(out_part.astype(jnp.bfloat16), 'ctx', scatter_dimension=...  72.8 us
    mul x2, other arithmetic, on_device(): qkv_weight.reshape(row_blocks, BLOCK, 3, col_blocks, BLOCK)  54.1 us
    unnamed x31, local copies, waits for them, and re-layouts  37.1 us
    reduce_scatter x1, waiting for transfers between devices, on_device(): lax.psum_scatter(jnp.einsum('tc,mc->tm', grad_proj, qkv_used, preferred_e...  29.7 us
    all_gather x1, waiting for transfers between devices, carried_in(): gathered = lax.all_gather(value.astype(jnp.bfloat16), axis)  23.8 us
  transfers between devices with their start and end apart: 8, of which 5 were waited for; matrix products, arithmetic and copies ran while one was open for 43% of the time, Pallas kernels for 0%

commit v1 on v0

--- a/solution.py
+++ b/solution.py
@@ -6,6 +6,28 @@
 
 BLOCK = 128
 EPSILON = 1e-05
+
+
+def joined_along(pieces, dim):
+    shape = list(pieces.shape[1:])
+    shape[dim] *= pieces.shape[0]
+    return jnp.moveaxis(pieces, 0, dim).reshape(shape)
+
+
+def collect(x, axis, dim):
+    size = lax.axis_size(axis)
+    pairs = [(i, (i + 1) % size) for i in range(size)]
+    back = [(b, a) for a, b in pairs]
+    lower, upper = ([], [])
+    for turn in range(size - 1):
+        if turn % 2 == 0:
+            lower.append(lax.ppermute(lower[-1] if lower else x, axis, pairs))
+        else:
+            upper.append(lax.ppermute(upper[-1] if upper else x, axis, back))
+    tiles = jnp.stack([*lower[::-1], x, *upper])
+    shift = lax.axis_index(axis) - len(lower)
+    tiles = tiles[(jnp.arange(size) - shift) % size]
+    return joined_along(tiles, dim)
 
 
 def carried_in(value, axis, join, neutral):
@@ -102,7 +124,7 @@
         tiled=True,
     ).astype(jnp.float32)
     layer_out = (tokens.astype(jnp.float32) + head_sum).astype(jnp.bfloat16)
-    grad_rows = lax.all_gather(cotangent, "tp", axis=0, tiled=True)
+    grad_rows = collect(cotangent, "tp", 0)
     ctx_count = lax.axis_size("ctx")
     ctx_place = lax.axis_index("ctx")
     slice_rows = model_width // ctx_count

time: 775 us -> 726 us (0.937)
  waiting for transfers between devices: 364 us -> 300 us
  other arithmetic: 83.5 us -> 93.5 us
  matrix products: 122 us -> 113 us
    all_gather x1 -> x0, waiting for transfers between devices: 78.7 us -> none  [on_device(): grad_rows = lax.all_gather(cotangent, 'tp', axis=0, tiled=True)]
    ppermute x0 -> x3, waiting for transfers between devices: none -> 36.9 us  [the longest x2 23.3 us: collect(): lower.append(lax.ppermute(lower[-1] if lower else x, axis, pairs))]
    all_gather x1, waiting for transfers between devices: 23.8 us -> 0.01 us  [carried_in(): gathered = lax.all_gather(value.astype(jnp.bfloat16), axis)]
    mul x0 -> x1, other arithmetic: none -> 8.95 us  [on_device(): out_weight.reshape(col_blocks, BLOCK, row_blocks, BLOCK)]
    unnamed x31 -> x32, local copies, waits for them, and re-layouts: 37.1 us -> 38.9 us
  transfers between devices with their start and end apart: 8 -> 10, of which waited for: 5 -> 5; matrix products, arithmetic and copies ran while one was open for 43% -> 50% of each run, Pallas kernels for 0% -> 0%
where the time goes in v1:
time: 726 us; the launch traced here: 714 us
  waiting for transfers between devices  300 us (41%)
  local copies, waits for them, and re-layouts  186 us (26%)
  matrix products  113 us (16%)
  other arithmetic  93.5 us (13%)
  between operations  14.6 us (2%)
    reduce_scatter x1, waiting for transfers between devices, on_device(): lax.psum_scatter(qkv_part.astype(jnp.bfloat16), 'ctx', scatter_dimension=...  157 us
    mul x5, local copies, waits for them, and re-layouts, on_device(): qkv_weight.reshape(row_blocks, BLOCK, 3, col_blocks, BLOCK)  124 us
    reduce_scatter x1, waiting for transfers between devices, on_device(): lax.psum_scatter(out_part.astype(jnp.bfloat16), 'ctx', scatter_dimension=...  72.7 us
    mul x2, other arithmetic, on_device(): qkv_weight.reshape(row_blocks, BLOCK, 3, col_blocks, BLOCK)  54.3 us
    unnamed x32, local copies, waits for them, and re-layouts  38.9 us
    reduce_scatter x1, waiting for transfers between devices, on_device(): lax.psum_scatter(jnp.einsum('tc,mc->tm', grad_proj, qkv_used, preferred_e...  32.6 us
    ppermute x2, waiting for transfers between devices, collect(): lower.append(lax.ppermute(lower[-1] if lower else x, axis, pairs))  23.3 us
    dot_general x1, matrix products, on_device(): jnp.einsum('tc,mc->tm', grad_proj, qkv_used, preferred_element_type=jnp.f...  19.6 us
  transfers between devices with their start and end apart: 10, of which 5 were waited for; matrix products, arithmetic and copies ran while one was open for 50% of the time, Pallas kernels for 0%

profile of v1, /device:TPU:0, one launch (start us, length us, event | category | flops | bytes accessed | tf_op | source)
XLA Modules:
  0.0 713.6 jit_solution(16860453401116775030)
XLA Ops:
  7.9 3.1 collective-permute-start
  11.8 8.9 %mul.111 = bf16[32,128,3,8,128]{4,3,2,1,0:T(8,128)(2,1)} broadcast(bf16[32,3,8]{2,1,0:T(4,128)(2,1)S(1)} %copy.51), dimensions={0,2,3} | broadcast | bytes 25167360 | tf_op jit(solution)/shard_map/mul | solution.py:90
  20.7 37.3 %mul.112 = bf16[4096,3072]{1,0:T(8,128)(2,1)} reshape(bf16[32,128,3,8,128]{4,3,2,1,0:T(8,128)(2,1)} %mul.111) | data formatting | bytes 50331648 | tf_op jit(solution)/shard_map/mul | solution.py:90
  58.0 31.6 %copy.52 = bf16[4096,3072]{0,1:T(8,128)(2,1)} copy(bf16[4096,3072]{1,0:T(8,128)(2,1)} %mul.112) | data formatting | bytes 50331648 | tf_op jit(solution)/shard_map/mul | solution.py:90
  89.6 33.6 %copy.50 = bf16[4096,3,1024]{0,2,1:T(8,128)(2,1)} copy(bf16[4096,3,1024]{2,0,1:T(8,128)(2,1)} %param.15) | data formatting | bytes 50331648 | tf_op args[3]
  123.2 25.4 %bitcast_multiply_fusion = bf16[4096,3072]{0,1:T(8,128)(2,1)} fusion(bf16[4096,3072]{0,1:T(8,128)(2,1)} %copy.52, bf16[4096,3,1024]{0,2,1:T(8,128)(2,1)} %copy.50), kind=kLoop, calls=%fused_computation.3 | loop fusion | flops 12582912 | bytes 75497472 | tf_op jit(solution)/shard_map/mul | solution.py:90
  148.7 18.2 %convolution_convert_fusion.3 = bf16[3072,512]{1,0:T(8,128)(2,1)S(1)} fusion(bf16[4096,3072]{0,1:T(8,128)(2,1)} %bitcast_multiply_fusion, bf16[512,4096]{1,0:T(8,128)(2,1)} %all-gather.6.cloned.1.call-done), kind=kOutput, calls=%fused_computation.12 | convolution fusion | flops 12886474752 | bytes 32505856 | tf_op jit(solution)/shard_map/dot_general | solution.py:97
  166.9 1.5 convolution_convert_fusion.4
  168.5 2.2 collective-permute-start.2
  170.8 1.1 mul.121
  172.0 9.0 %bitcast_multiply_fusion.1 = bf16[1024,4096]{1,0:T(8,128)(2,1)} fusion(bf16[1024,4096]{1,0:T(8,128)(2,1)} %param.17, bf16[128,8,32,128]{3,2,1,0:T(8,128)(2,1)S(1)} %bitcast.141), kind=kLoop, calls=%fused_computation.5 | loop fusion | flops 4194304 | bytes 25165824 | tf_op jit(solution)/shard_map/mul | solution.py:93
  180.9 13.6 %collective-permute-done.2 = bf16[128,4096]{1,0:T(8,128)(2,1)} collective-permute-done((bf16[128,4096]{1,0:T(8,128)(2,1)}, bf16[128,4096]{1,0:T(8,128)(2,1)}, u32[]{:S(2)}, u32[]{:S(2)}) %collective-permute-start.2) | collective-permute-done | bytes 1048608 | tf_op jit(solution)/shard_map/ppermute | solution.py:26
  194.5 23.3 %collective-permute-done.1 = bf16[128,4096]{1,0:T(8,128)(2,1)S(1)} collective-permute-done((bf16[128,4096]{1,0:T(8,128)(2,1)}, bf16[128,4096]{1,0:T(8,128)(2,1)S(1)}, u32[]{:S(2)}, u32[]{:S(2)}) %collective-permute-start.1) | collective-permute-done | bytes 1048608 | tf_op jit(solution)/shard_map/ppermute | solution.py:24
  217.8 3.5 pad_maximum_fusion
  221.3 5.0 gather_fusion
  226.3 1.4 select_convert_fusion.1
  227.7 2.0 copy-done.2
  229.7 2.8 fusion.11
  232.7 3.2 fusion.4
  236.0 7.0 multiply_reduce_fusion
  243.0 1.6 subtract_multiply_fusion
  244.6 3.1 convolution_convert_fusion.5
  247.8 10.3 %convolution_convert_fusion.2 = bf16[512,4096]{1,0:T(8,128)(2,1)} fusion(bf16[512,1024]{0,1:T(8,128)(2,1)} %bitcast.161, bf16[1024,4096]{1,0:T(8,128)(2,1)} %bitcast_multiply_fusion.1), kind=kOutput, calls=%fused_computation.11 | convolution fusion | flops 4297064448 | bytes 13631488 | tf_op jit(solution)/shard_map/dot_general | solution.py:121
  258.3 8.8 %mul.111.clone = bf16[32,128,3,8,128]{1,0,4,3,2:T(8,128)(2,1)} broadcast(bf16[32,3,8]{0,2,1:T(8,128)(2,1)S(1)} %convert_bitcast_fusion.3), dimensions={0,2,3} | broadcast | bytes 25167360 | tf_op jit(solution)/shard_map/mul | solution.py:90
  267.1 37.6 %mul.132 = bf16[4096,3,1024]{0,2,1:T(8,128)(2,1)} reshape(bf16[32,128,3,8,128]{1,0,4,3,2:T(8,128)(2,1)} %mul.111.clone) | data formatting | bytes 50331648 | tf_op jit(solution)/shard_map/mul | solution.py:90
  304.8 28.8 %mul.133 = bf16[4096,3,1024]{0,2,1:T(8,128)(2,1)} multiply(bf16[4096,3,1024]{0,2,1:T(8,128)(2,1)} %copy.50, bf16[4096,3,1024]{0,2,1:T(8,128)(2,1)} %mul.132) | non-fusion elementwise | flops 12582912 | bytes 75497472 | tf_op jit(solution)/shard_map/mul | solution.py:90
  333.6 2.7 select_convert_fusion
  336.3 1.5 fusion.21
  337.8 2.9 fusion.7
  340.7 2.2 fusion.16
  343.6 2.0 fusion.12
  345.7 8.1 %while.23 = (s32[]{:T(128)}, f32[8,128,128]{2,1,0:T(8,128)S(1)}, s32[]{:T(128)}, bf16[8,8,128,128]{3,2,1,0:T(8,128)(2,1)}, s32[]{:T(128)}, /*index=5*/s32[]{:T(128)}, s32[]{:T(128)}, s32[]{:T(128)}) while((s32[]{:T(128)}, f32[8,128,128]{2,1,0:T(8,128)S(1)}, s32[]{:T(128)}, bf16[8,8,128,128]{3,2,1,0:T(8,128)(2,1)}, s32[]{:T(128)}, ...), condition=%wide.region_6.7_spmd, body=%wide.region_5.6_spmd.sunk | while | flops 262150 | bytes 1310863 | solution.py:57
  353.8 3.1 fusion.6
  356.9 2.4 fusion.8
  359.7 19.6 %convolution_convert_fusion.1 = bf16[512,4096]{1,0:T(8,128)(2,1)} fusion(bf16[512,3072]{0,1:T(8,128)(2,1)S(1)} %bitcast.158, bf16[4096,3072]{0,1:T(8,128)(2,1)} %bitcast.142), kind=kOutput, calls=%fused_computation.10 | convolution fusion | flops 12886999040 | bytes 32505856 | tf_op jit(solution)/shard_map/tc,mc->tm/dot_general | solution.py:185
  379.6 10.3 %convolution_convert_fusion = bf16[4096,1024]{1,0:T(8,128)(2,1)} fusion(bf16[512,4096]{1,0:T(8,128)(2,1)} %bitcast.155, bf16[512,1024]{0,1:T(8,128)(2,1)} %bitcast.162), kind=kOutput, calls=%fused_computation.8 | convolution fusion | flops 4299161600 | bytes 13631488 | tf_op jit(solution)/shard_map/tm,tf->mf/dot_general | solution.py:133
  390.0 19.0 %convert_bitcast_fusion = bf16[4096,3072]{0,1:T(8,128)(2,1)} fusion(bf16[512,3072]{0,1:T(8,128)(2,1)S(1)} %bitcast.159, bf16[512,4096]{1,0:T(8,128)(2,1)} %all-gather.6.cloned.1.call-done), kind=kOutput, calls=%fused_computation.4 | convolution fusion | flops 12897484800 | bytes 32505856 | tf_op jit(solution)/shard_map/tm,tc->mc/dot_general | solution.py:174
  409.9 3.2 broadcast_in_dim.21
  413.1 7.2 %reshape.127 = f32[512,3,1024]{2,0,1:T(8,128)} reshape(f32[4,128,3,8,128]{4,3,1,0,2:T(8,128)} %broadcast_in_dim.21) | data formatting | bytes 12582912 | tf_op jit(solution)/shard_map/reshape | solution.py:182
  420.4 2.5 add_convert_fusion.2
  423.0 32.6 %reduce-scatter.7.cloned.1.call-done = bf16[128,4096]{1,0:T(8,128)(2,1)} async-done(((bf16[512,4096]{1,0:T(8,128)(2,1)}), bf16[128,4096]{1,0:T(8,128)(2,1)}) %reduce-scatter.7.cloned.1.call-update) | async-done | bytes 1048592 | tf_op jit(solution)/shard_map/reduce_scatter | solution.py:184
  455.6 2.4 add_convert_fusion
  458.0 72.7 %reduce-scatter.11.cloned.1.call-done = bf16[512,1024]{1,0:T(8,128)(2,1)} async-done(((bf16[4096,1024]{1,0:T(8,128)(2,1)}), bf16[512,1024]{1,0:T(8,128)(2,1)}) %reduce-scatter.11.cloned.1.call-update) | async-done | bytes 1048592 | tf_op jit(solution)/shard_map/reduce_scatter | solution.py:134
  530.9 1.9 fusion.1
  532.8 1.8 copy.70
  534.6 157.0 %reduce-scatter.9.cloned.1.call-done = bf16[512,3072]{0,1:T(8,128)(2,1)} async-done(((bf16[4096,3072]{0,1:T(8,128)(2,1)}), bf16[512,3072]{0,1:T(8,128)(2,1)}) %reduce-scatter.9.cloned.1.call-update) | async-done | bytes 3145744 | tf_op jit(solution)/shard_map/reduce_scatter | solution.py:175
  691.6 5.4 copy.68
  697.0 9.5 %multiply_multiply_fusion = f32[512,3,1024]{2,0,1:T(8,128)} fusion(f32[512,3,1024]{2,0,1:T(8,128)} %copy.68, f32[512,3,1024]{2,0,1:T(8,128)} %reshape.127), kind=kLoop, calls=%fused_computation.9 | loop fusion | flops 3145728 | bytes 18874368 | tf_op jit(solution)/shard_map/mul | solution.py:183
  (75 shorter events, 12.6 us)
Async XLA Ops:
  7.2 141.5 %all-gather.6.cloned.1.call-start = ((), (), s32[]{:S(2)}) async-start(), calls=%async_computation.4 | async-start | bytes 5242880 | tf_op jit(solution)/shard_map/all_gather | solution.py:96
  7.9 224.6 %all-gather.8.cloned.1.call-start = ((), (), s32[]{:S(2)}) async-start(), calls=%async_computation.9 | async-start | bytes 2359296 | tf_op jit(solution)/shard_map/all_gather | solution.py:35
  7.9 162.8 %collective-permute-start = (bf16[128,4096]{1,0:T(8,128)(2,1)}, bf16[128,4096]{1,0:T(8,128)(2,1)}, u32[]{:S(2)}, u32[]{:S(2)}) collective-permute-start(bf16[128,4096]{1,0:T(8,128)(2,1)} %param.19), channel_id=1, source_target_pairs={{0,1},{1,2},{2,3},{3,0},{4,5},{5,6},{6,7},{7,4},{8,9},{9,10},{10,1... | collective-permute-start | bytes 3145736 | tf_op jit(solution)/shard_map/ppermute | solution.py:24
  89.6 33.6 %copy-start.11 = (s32[512,8]{0,1:T(8,128)S(1)}, s32[512,8]{0,1:T(8,128)}, u32[]{:S(2)}) copy-start(s32[512,8]{0,1:T(8,128)} %param.13) | copy-start | bytes 49156
  89.6 33.6 %copy-start.12 = (s32[512,8]{0,1:T(8,128)S(1)}, s32[512,8]{0,1:T(8,128)}, u32[]{:S(2)}) copy-start(s32[512,8]{0,1:T(8,128)} %param.14) | copy-start | bytes 49156
  166.9 60.8 %copy-start = (bf16[3072,512]{1,0:T(8,128)(2,1)}, bf16[3072,512]{1,0:T(8,128)(2,1)S(1)}, u32[]{:S(2)}) copy-start(bf16[3072,512]{1,0:T(8,128)(2,1)S(1)} %convolution_convert_fusion.3) | copy-start | bytes 9437188
  166.9 3.8 copy-start.13
  168.4 177.3 %all-gather.10.cloned.1.call-start = ((), (), s32[]{:S(2)}) async-start(), calls=%async_computation.10 | async-start | bytes 2359296 | tf_op jit(solution)/shard_map/all_gather | solution.py:48
  168.5 26.1 %collective-permute-start.2 = (bf16[128,4096]{1,0:T(8,128)(2,1)}, bf16[128,4096]{1,0:T(8,128)(2,1)}, u32[]{:S(2)}, u32[]{:S(2)}) collective-permute-start(bf16[128,4096]{1,0:T(8,128)(2,1)} %param.19), channel_id=1, source_target_pairs={{1,0},{2,1},{3,2},{0,3},{5,4},{6,5},{7,6},{4,7},{9,8},{10,9},{11,1... | collective-permute-start | bytes 3145736 | tf_op jit(solution)/shard_map/ppermute | solution.py:26
  170.8 47.0 %collective-permute-start.1 = (bf16[128,4096]{1,0:T(8,128)(2,1)}, bf16[128,4096]{1,0:T(8,128)(2,1)S(1)}, u32[]{:S(2)}, u32[]{:S(2)}) collective-permute-start(bf16[128,4096]{1,0:T(8,128)(2,1)} %collective-permute-done), channel_id=1, source_target_pairs={{0,1},{1,2},{2,3},{3,0},{4,5},{5,6},{6,7},{7,4},{8,9},{9,10},{10,1... | collective-permute-start | bytes 3145736 | tf_op jit(solution)/shard_map/ppermute | solution.py:24
  172.0 45.8 %copy-start.7 = (bf16[128,4096]{1,0:T(8,128)(2,1)S(1)}, bf16[128,4096]{1,0:T(8,128)(2,1)}, u32[]{:S(2)}) copy-start(bf16[128,4096]{1,0:T(8,128)(2,1)} %param.19) | copy-start | bytes 3145732
  227.7 2.0 copy-start.2
  232.7 3.3 copy-start.6
  247.8 172.7 %reduce-scatter.5.cloned.1.call-start = ((), (), s32[]{:S(2)}) async-start(), calls=%async_computation.5 | async-start | bytes 5242880 | tf_op jit(solution)/shard_map/reduce_scatter | solution.py:120
  258.1 197.5 %reduce-scatter.7.cloned.1.call-start = ((), (), s32[]{:S(2)}) async-start(), calls=%async_computation.6 | async-start | bytes 5242880 | tf_op jit(solution)/shard_map/reduce_scatter | solution.py:184
  333.6 2.7 copy-start.1
  340.7 2.9 copy-start.3
  353.8 3.2 copy-start.4
  356.9 2.5 copy-start.9
  379.3 151.3 %reduce-scatter.11.cloned.1.call-start = ((), (), s32[]{:S(2)}) async-start(), calls=%async_computation.8 | async-start | bytes 9437184 | tf_op jit(solution)/shard_map/reduce_scatter | solution.py:134
  389.9 301.7 %reduce-scatter.9.cloned.1.call-start = ((), (), s32[]{:S(2)}) async-start(), calls=%async_computation.7 | async-start | bytes 28311552 | tf_op jit(solution)/shard_map/reduce_scatter | solution.py:175
  409.0 0.7 copy-start.10
  413.1 7.2 %copy-start.14 = (s32[8,32]{1,0:T(8,128)S(1)}, s32[8,32]{1,0:T(8,128)}, u32[]{:S(2)}) copy-start(s32[8,32]{1,0:T(8,128)} %param.18) | copy-start | bytes 3076
  413.1 7.4 %copy-start.5 = (bf16[128,4096]{1,0:T(8,128)(2,1)S(1)}, bf16[128,4096]{1,0:T(8,128)(2,1)}, u32[]{:S(2)}) copy-start(bf16[128,4096]{1,0:T(8,128)(2,1)} %param.12) | copy-start | bytes 3145732
  420.3 35.3 %copy-start.8 = (bf16[128,4096]{1,0:T(8,128)(2,1)S(1)}, bf16[128,4096]{1,0:T(8,128)(2,1)}, u32[]{:S(2)}) copy-start(bf16[128,4096]{1,0:T(8,128)(2,1)} %param.19) | copy-start | bytes 3145732
Sparse Core Ops, SparseCore 0:
  9.6 95.0 all-gather.5
  168.5 27.9 all-gather.7
  247.9 34.4 all-gather.9
  284.5 76.7 reduce-scatter.4
  379.5 76.0 reduce-scatter.6
  458.9 71.7 reduce-scatter.10
  534.7 156.8 reduce-scatter.8
